TPU v7x, 256 devices: a whole 4x4x8 slice. The times are simulated.
256 devices in a mesh: seq: 64 (over z, x, core), tp: 4 (over y).
Axes of the slice: x: 4, y: 4, z: 8, core: 2. Of those that a mesh axis runs over, the one named last changes fastest.
Arguments:
- hidden: bfloat16 [8192, 1024], P('seq'), may hold values from -120 to 120
- page_table: int32 [16, 256], replicated, may hold values from -1 to 2111, as said below
- cache_len: int32 [16], replicated, may hold values from 129 to 32768, as said below
- expert_ids: int32 [8192, 2], P('seq'), may hold values from 0 to 31, all different within a row; in each aligned block of 128 rows (0 to 127, 128 to 255, ...) at most 10 rows name the same one
- w_query: bfloat16 [1024, 1024], P(None, 'tp'), may hold values from -4 to 4
- w_key: bfloat16 [1024, 1024], P(None, 'tp'), may hold values from -0.1875 to 0.1875
- w_value: bfloat16 [1024, 1024], P(None, 'tp'), may hold values from -0.1875 to 0.1875
- w_out: bfloat16 [1024, 1024], P('tp'), may hold values from -0.1875 to 0.1875
- cache_k: bfloat16 [2112, 128, 1024], P('seq', None, 'tp'), may hold values from -4000 to 4000
- cache_v: bfloat16 [2112, 128, 1024], P('seq', None, 'tp'), may hold values from -6 to 6
- moe_gain: float32 [1024], replicated, may hold values from 0.1 to 1.9
- router: float32 [1024, 32], replicated, may hold values from -0.1875 to 0.1875
- w_gate_up: bfloat16 [64, 2, 1024, 1408], P('seq', None, None, 'tp'), may hold values from -0.1875 to 0.1875
- w_down: bfloat16 [64, 1408, 1024], P('seq', 'tp'), may hold values from -0.109375 to 0.109375
Outputs:
- out: bfloat16 [8192, 1024], P('seq', 'tp')
Inputs may be any that keep to these rules, and one draw needn't show every extreme that they name: `page_table`: row r lists the pages of request r's cache in order, ceil(cache_len[r] / 128) of them, then -1; no page number appears twice in the table. `cache_len`: half of the requests have exactly 32768 cached tokens; the others have at most 384. `expert_ids`: A token names 2 different experts; among the 128 tokens of one device no expert is named more than 10 times, and on some device one expert is named exactly 10 times.
All inputs are finite; a program needn't handle non-finite values.
Results may differ from a plain program's by a relative error of at most 0.0085.
Values may be sent and summed in bfloat16 or wider, within the bound.
No kernel may reach another device: no remote copies, remote signals or barrier semaphores. Data moves between devices by JAX's collectives and lax.ppermute only.
A program may use at most 128 MiB of HBM per device.

v0:
```python
import jax
import jax.numpy as jnp
from jax import lax
from jax.sharding import PartitionSpec as P

DH = 64
EXPERTS = 32
TOP = 2
PAGE = 128
MAXP = 256
SPAN_DEVS = 4
CAP = 10
NEGATIVE = -1e30


def passed_along(value, axis, steps):
    count = lax.axis_size(axis)
    pairs = [(source, (source + steps) % count) for source in range(count)]
    return lax.ppermute(value, axis, pairs)


def rms_rows(values):
    return values * lax.rsqrt(jnp.mean(values * values, axis=-1, keepdims=True) + 1e-06)


def online_update(state, queries, keys, values, mask):
    m_old, l_old, accum = state
    scale = queries.shape[2] ** (-0.5)
    scores = jnp.einsum("nhd,khd->hnk", queries, keys, preferred_element_type=jnp.float32) * scale
    scores = jnp.where(mask[None], scores, NEGATIVE)
    m_new = jnp.maximum(m_old, jnp.max(scores, axis=-1).T)
    probs = jnp.where(mask[None], jnp.exp(scores - m_new.T[:, :, None]), 0.0)
    factor = jnp.exp(m_old - m_new)
    l_new = l_old * factor + jnp.sum(probs, axis=-1).T
    weighted = jnp.einsum(
        "hnk,khd->nhd", probs.astype(jnp.bfloat16), values, preferred_element_type=jnp.float32
    )
    return (m_new, l_new, accum * factor[:, :, None] + weighted)


def shards(
    hidden,
    page_table,
    cache_len,
    expert_ids,
    w_query,
    w_key,
    w_value,
    w_out,
    cache_k,
    cache_v,
    moe_gain,
    router,
    w_gate_up,
    w_down,
):
    tok_rows = hidden.shape[0]
    span_rows = tok_rows * SPAN_DEVS
    seq_count = lax.axis_size("seq")
    seq_index = lax.axis_index("seq")
    local_heads = w_query.shape[1] // DH
    request_total = page_table.shape[0]
    normed = rms_rows(hidden.astype(jnp.float32)).astype(jnp.bfloat16)
    queries = jnp.dot(normed, w_query, preferred_element_type=jnp.float32).astype(jnp.bfloat16)
    new_keys = (
        jnp.dot(normed, w_key, preferred_element_type=jnp.float32)
        .astype(jnp.bfloat16)
        .reshape(tok_rows, local_heads, DH)
    )
    new_values = (
        jnp.dot(normed, w_value, preferred_element_type=jnp.float32)
        .astype(jnp.bfloat16)
        .reshape(tok_rows, local_heads, DH)
    )
    page_count = cache_k.shape[0]
    page_ids = seq_index * page_count + jnp.arange(page_count, dtype=jnp.int32)
    listing = page_table.reshape(-1)
    matches = listing[None, :] == page_ids[:, None]
    entry_index = jnp.arange(listing.shape[0], dtype=jnp.int32)
    found = jnp.sum(jnp.where(matches, entry_index[None, :] + 1, 0), axis=1) - 1
    page_owner = jnp.where(found >= 0, found // MAXP, -1)
    page_order = jnp.where(found >= 0, found % MAXP, 0)
    page_limit = jnp.where(found >= 0, cache_len[jnp.maximum(page_owner, 0)], 0)
    own_request = seq_index * tok_rows // span_rows
    own_offset = seq_index * tok_rows % span_rows
    slot_range = jnp.arange(PAGE, dtype=jnp.int32)
    page_valid = (found >= 0)[:, None] & (
        page_order[:, None] * PAGE + slot_range[None, :] < page_limit[:, None]
    )
    span_positions = jnp.arange(span_rows, dtype=jnp.int32)
    fresh_mask = (
        span_positions[:, None] >= own_offset + jnp.arange(tok_rows, dtype=jnp.int32)[None, :]
    )
    mask = jnp.concatenate(
        [jnp.broadcast_to(page_valid[:, None, :], (page_count, span_rows, PAGE)), fresh_mask[None]],
        axis=0,
    )
    owners = jnp.concatenate([page_owner, own_request[None]], axis=0)
    keys = jnp.concatenate(
        [cache_k.reshape(page_count, PAGE, local_heads, DH), new_keys[None]], axis=0
    )
    values = jnp.concatenate(
        [cache_v.reshape(page_count, PAGE, local_heads, DH), new_values[None]], axis=0
    )
    everyone = lax.all_gather(queries, "seq", axis=0, tiled=True).reshape(
        request_total, span_rows, local_heads, DH
    )
    rows = everyone[jnp.maximum(owners, 0)]
    scores = jnp.einsum("bqhd,bkhd->bhqk", rows, keys, preferred_element_type=jnp.float32) * DH ** (
        -0.5
    )
    scores = jnp.where(mask[:, None], scores, NEGATIVE)
    m_block = jnp.max(scores, axis=-1)
    probs = jnp.where(mask[:, None], jnp.exp(scores - m_block[..., None]), 0.0)
    l_block = jnp.sum(probs, axis=-1)
    acc_block = jnp.einsum(
        "bhqk,bkhd->bhqd", probs.astype(jnp.bfloat16), values, preferred_element_type=jnp.float32
    )
    onehot = owners[:, None] == jnp.arange(request_total, dtype=jnp.int32)[None, :]
    m_local = jnp.max(jnp.where(onehot[:, :, None, None], m_block[:, None], NEGATIVE), axis=0)
    factor = jnp.exp(m_block - m_local[jnp.maximum(owners, 0)])
    weights = onehot.astype(jnp.float32)
    acc_req = jnp.einsum(
        "br,bhqd->rhqd", weights, acc_block * factor[..., None], precision=lax.Precision.HIGHEST
    )
    l_req = jnp.einsum("br,bhq->rhq", weights, l_block * factor, precision=lax.Precision.HIGHEST)
    quarters = span_rows // tok_rows
    acc_req = jnp.transpose(
        acc_req.reshape(request_total, local_heads, quarters, tok_rows, DH), (0, 2, 1, 3, 4)
    )
    stats = jnp.stack([m_local, l_req], axis=-1)
    stats = jnp.transpose(
        stats.reshape(request_total, local_heads, quarters, tok_rows, 2), (0, 2, 1, 3, 4)
    )
    bit_count = seq_count.bit_length() - 1
    acc_req = acc_req.reshape((2,) * bit_count + acc_req.shape[2:])
    stats = stats.reshape((2,) * bit_count + stats.shape[2:])
    remaining = list(range(bit_count - 1, -1, -1))
    for bit in [0, 1, 3, 2, 4, 5] if bit_count == 6 else list(range(bit_count)):
        axis = remaining.index(bit)
        remaining.pop(axis)
        own_bit = seq_index >> bit & 1
        keep_acc = lax.dynamic_index_in_dim(acc_req, own_bit, axis, keepdims=False)
        send_acc = lax.dynamic_index_in_dim(acc_req, 1 - own_bit, axis, keepdims=False)
        keep_stats = lax.dynamic_index_in_dim(stats, own_bit, axis, keepdims=False)
        send_stats = lax.dynamic_index_in_dim(stats, 1 - own_bit, axis, keepdims=False)
        pairs = [(source, source ^ 1 << bit) for source in range(seq_count)]
        got_acc = lax.ppermute(send_acc.astype(jnp.bfloat16), "seq", pairs).astype(jnp.float32)
        got_stats = lax.ppermute(send_stats, "seq", pairs)
        m_new = jnp.maximum(keep_stats[..., 0], got_stats[..., 0])
        keep_factor = jnp.exp(keep_stats[..., 0] - m_new)
        got_factor = jnp.exp(got_stats[..., 0] - m_new)
        l_new = keep_stats[..., 1] * keep_factor + got_stats[..., 1] * got_factor
        acc_req = keep_acc * keep_factor[..., None] + got_acc * got_factor[..., None]
        stats = jnp.stack([m_new, l_new], axis=-1)
    attention = jnp.transpose(acc_req / stats[..., 1:2], (1, 0, 2)).reshape(tok_rows, -1)
    attention = attention.astype(jnp.bfloat16)
    tp_count = lax.axis_size("tp")
    tp_index = lax.axis_index("tp")

    def tp_gather(value, axis):
        pieces = [value] + [
            lax.ppermute(value, "tp", [(i, (i + k) % tp_count) for i in range(tp_count)])
            for k in range(1, tp_count)
        ]
        stacked = jnp.stack(pieces, axis=0)
        ordered = jnp.take(stacked, (tp_index - jnp.arange(tp_count)) % tp_count, axis=0)
        return jnp.concatenate([ordered[j] for j in range(tp_count)], axis=axis)

    full_attention = tp_gather(attention, 1)
    full_w_out = tp_gather(w_out, 0)
    mid = hidden.astype(jnp.float32) + jnp.dot(
        full_attention, full_w_out, preferred_element_type=jnp.float32
    )
    moe_in = (rms_rows(mid) * moe_gain).astype(jnp.bfloat16)
    logits = jnp.dot(moe_in.astype(jnp.float32), router, precision=lax.Precision.HIGHEST)
    chosen = jax.nn.sigmoid(jnp.take_along_axis(logits, expert_ids, axis=1))
    gates = chosen / jnp.sum(chosen, axis=1, keepdims=True)
    flat_ids = expert_ids.reshape(-1)
    onehot = (flat_ids[:, None] == jnp.arange(EXPERTS, dtype=jnp.int32)[None, :]).astype(jnp.int32)
    ranks = jnp.sum((jnp.cumsum(onehot, axis=0) - 1) * onehot, axis=1)
    target = (flat_ids * CAP + ranks).reshape(tok_rows, TOP)
    hits = target[:, :, None] == jnp.arange(EXPERTS * CAP, dtype=jnp.int32)[None, None, :]
    placing = jnp.any(hits, axis=1).astype(jnp.bfloat16)
    combining = jnp.sum(jnp.where(hits, gates[:, :, None], 0.0), axis=1)
    packed = jnp.einsum("te,td->ed", placing, moe_in, preferred_element_type=jnp.float32).astype(
        jnp.bfloat16
    )
    width = moe_in.shape[1]
    splits = max(1, seq_count // EXPERTS)
    per_device = w_gate_up.shape[0]
    outgoing = jnp.repeat(packed.reshape(EXPERTS, CAP, width), splits, axis=0).reshape(
        seq_count, per_device, CAP, width
    )
    received = lax.all_to_all(outgoing, "seq", split_axis=0, concat_axis=0, tiled=True)
    count = received.shape[2]
    rows = received[:, 0].reshape(-1, width)
    gate = jnp.dot(rows, w_gate_up[0, 0], preferred_element_type=jnp.float32)
    upper = jnp.dot(rows, w_gate_up[0, 1], preferred_element_type=jnp.float32)
    inner = (jax.nn.gelu(gate, approximate=True) * upper).astype(jnp.bfloat16)
    results = [
        jnp.dot(inner, w_down[0], preferred_element_type=jnp.float32).reshape(
            seq_count, count, width
        )
    ]
    produced = jnp.stack(results, axis=1)
    returned = lax.all_to_all(
        produced.astype(jnp.bfloat16), "seq", split_axis=0, concat_axis=0, tiled=True
    ).astype(produced.dtype)
    columns = returned.shape[3]
    folded = jnp.sum(returned.reshape(EXPERTS, splits, CAP, columns), axis=1).reshape(
        EXPERTS * CAP, columns
    )
    mixture = jnp.dot(combining, folded, precision=lax.Precision.HIGHEST)
    tp_width = width // lax.axis_size("tp")
    mid_part = lax.dynamic_slice_in_dim(mid, lax.axis_index("tp") * tp_width, tp_width, 1)
    moe_part = lax.psum_scatter(
        mixture.astype(jnp.bfloat16), "tp", scatter_dimension=1, tiled=True
    ).astype(jnp.float32)
    return (mid_part + moe_part).astype(jnp.bfloat16)


def solution(mesh):
    in_specs = (
        P("seq", None),
        P(),
        P(),
        P("seq", None),
        P(None, "tp"),
        P(None, "tp"),
        P(None, "tp"),
        P("tp", None),
        P("seq", None, "tp"),
        P("seq", None, "tp"),
        P(),
        P(),
        P("seq", None, None, "tp"),
        P("seq", "tp", None),
    )
    out_specs = P("seq", "tp")
    return jax.shard_map(shards, mesh=mesh, in_specs=in_specs, out_specs=out_specs, check_vma=False)
```

profile of v0, /device:TPU:2, one launch (start us, length us, event | category | flops | bytes accessed | tf_op | source)
XLA Modules:
  0.0 483.9 jit_solution(15697876299836480089)
XLA Ops:
  11.5 2.9 collective-permute-start.16
  19.3 2.4 copy.110
  25.6 4.1 copy.112
  34.2 56.6 %all-gather.2.cloned.1.call-done = bf16[8192,256]{1,0:T(8,128)(2,1)} async-done(((bf16[128,256]{1,0:T(8,128)(2,1)}), bf16[8192,256]{1,0:T(8,128)(2,1)}) %all-gather.2.cloned.1.call-update) | async-done | bytes 4194320 | tf_op jit(solution)/shard_map/all_gather | solution.py:105
  90.8 13.0 %reshape.474 = bf16[16,512,4,64]{3,2,1,0:T(4,128)(2,1)} reshape(bf16[8192,256]{1,0:T(8,128)(2,1)} %all-gather.2.cloned.1.call-done) | data formatting | bytes 8388608 | tf_op jit(solution)/shard_map/reshape | solution.py:105
  103.8 12.7 %copy.109 = bf16[16,512,4,64]{1,3,2,0:T(8,128)(2,1)} copy(bf16[16,512,4,64]{3,2,1,0:T(4,128)(2,1)} %reshape.474) | data formatting | bytes 8388608 | tf_op jit(solution)/shard_map/reshape | solution.py:105
  116.5 7.5 %gather_fusion.1 = bf16[34,512,4,64]{1,3,2,0:T(8,128)(2,1)} fusion(bf16[16,512,4,64]{1,3,2,0:T(8,128)(2,1)} %copy.109, s32[1024]{0:T(1024)S(1)} %pad_clamp_fusion.1), kind=kCustom, calls=%fused_computation.1 | custom fusion | bytes 17825928 | tf_op jit(solution)/shard_map/gather | solution.py:108
  124.0 17.1 %fusion = (f32[34,4,512]{2,1,0:T(4,128)S(1)}, f32[34,4,512,128]{2,3,1,0:T(8,128)}) fusion(pred[34,512,128]{1,2,0:T(8,128)(4,1)S(1)} %pad_add_fusion, bf16[34,512,4,64]{1,3,2,0:T(8,128)(2,1)} %gather_fusion.1, bf16[1,128,4,64]{1,3,2,0:T(8,128)(2,1)S(1)} %bitcast.238, bf16[33,128,4,64]{1,3,2,0:T(8,128)(2,1)} %bitcast.223), kind=kOutput, calls=%fused_computation.8 | convolution fusion | flops 1168633856 | bytes 49299456 | tf_op jit(solution)/shard_map/bqhd,bkhd->bhqk/dot_general | solution.py:109
  141.1 17.5 %fusion.1 = f32[34,4,512]{2,1,0:T(4,128)} fusion(f32[34,4,512,128]{2,3,1,0:T(8,128)} %get-tuple-element.56, f32[34,4,512]{2,1,0:T(4,128)S(1)} %get-tuple-element.55, pred[34,512,128]{1,2,0:T(8,128)(4,1)S(1)} %pad_add_fusion), kind=kLoop, calls=%fused_computation.9 | loop fusion | flops 44494848 | bytes 38436864 | tf_op jit(solution)/shard_map/reduce_sum | solution.py:115
  160.4 2.5 gather_fusion.2
  164.7 21.5 %broadcast_multiply_fusion = f32[34,4,512,64]{2,3,1,0:T(8,128)} fusion(f32[34,4,512]{2,1,0:T(4,128)S(1)} %bitcast.232, f32[34,4,512,128]{2,3,1,0:T(8,128)} %get-tuple-element.56, f32[34,4,512]{2,1,0:T(4,128)S(1)} %get-tuple-element.55, pred[34,512,128]{1,2,0:T(8,128)(4,1)S(1)} %pad_add_fusion, bf16[1,128,4,64]{1,3,2,0:T(8,128)(2,1)S(1)} %bitcast.239, ...), kind=kOutput, calls=%fused_computation.19 | convolution fusion | flops 1194328064 | bytes 58490880 | tf_op jit(solution)/shard_map/bhqk,bkhd->bhqd/dot_general | solution.py:116
  186.2 25.1 %fusion.3 = f32[16,4,512,64]{2,0,3,1:T(8,128)} fusion(f32[34,4,512,64]{2,3,1,0:T(8,128)} %broadcast_multiply_fusion, s32[34]{0:T(128)S(1)} %copy-done.18), kind=kOutput, calls=%fused_computation.11 | convolution fusion | flops 855638528 | bytes 26214536 | tf_op jit(solution)/shard_map/br,bhqd->rhqd/dot_general | solution.py:123
  211.3 10.3 %reshape.409 = f32[16,4,4,128,64]{3,2,0,4,1:T(4,128)} reshape(f32[16,4,512,64]{2,0,3,1:T(8,128)} %fusion.3) | data formatting | bytes 16777216 | tf_op jit(solution)/shard_map/reshape | solution.py:129
  221.6 8.2 %copy.118 = f32[16,4,4,128,64]{3,4,2,1,0:T(8,128)S(1)} copy(f32[16,4,4,128,64]{3,1,0,4,2:T(4,128)} %bitcast.217) | data formatting | bytes 16777216 | tf_op jit(solution)/shard_map/transpose | solution.py:128
  229.9 3.2 copy-done.2
  235.3 2.9 pad_maximum_fusion
  238.3 2.3 gather_fusion.4
  246.5 4.0 fusion.14
  252.0 3.1 collective-permute-done.4
  257.2 18.8 %collective-permute-done.3 = bf16[2,2,2,2,4,128,64]{5,6,4,3,2,1,0:T(8,128)(2,1)S(1)} collective-permute-done((bf16[2,2,2,2,4,128,64]{5,6,4,3,2,1,0:T(8,128)(2,1)S(1)}, bf16[2,2,2,2,4,128,64]{5,6,4,3,2,1,0:T(8,128)(2,1)S(1)}, u32[]{:S(2)}, u32[]{:S(2)}) %collective-permute-start.3) | collective-permute-done | bytes 1048608 | tf_op jit(solution)/shard_map/ppermute | solution.py:148
  279.7 10.2 %collective-permute-done.5 = bf16[2,2,2,4,128,64]{4,5,3,2,1,0:T(8,128)(2,1)S(1)} collective-permute-done((bf16[2,2,2,4,128,64]{4,5,3,2,1,0:T(8,128)(2,1)S(1)}, bf16[2,2,2,4,128,64]{4,5,3,2,1,0:T(8,128)(2,1)S(1)}, u32[]{:S(2)}, u32[]{:S(2)}) %collective-permute-start.5) | collective-permute-done | bytes 524320 | tf_op jit(solution)/shard_map/ppermute | solution.py:148
  291.1 3.0 collective-permute-start.10
  294.1 4.0 collective-permute-done.7
  300.4 5.3 %collective-permute-done.9 = bf16[2,4,128,64]{2,3,1,0:T(8,128)(2,1)S(1)} collective-permute-done((bf16[2,4,128,64]{2,3,1,0:T(8,128)(2,1)S(1)}, bf16[2,4,128,64]{2,3,1,0:T(8,128)(2,1)S(1)}, u32[]{:S(2)}, u32[]{:S(2)}) %collective-permute-start.9) | collective-permute-done | bytes 131104 | tf_op jit(solution)/shard_map/ppermute | solution.py:148
  305.8 3.0 collective-permute-start.11
  308.8 5.9 %collective-permute-done.11 = bf16[4,128,64]{1,2,0:T(8,128)(2,1)S(1)} collective-permute-done((bf16[4,128,64]{1,2,0:T(8,128)(2,1)S(1)}, bf16[4,128,64]{1,2,0:T(8,128)(2,1)S(1)}, u32[]{:S(2)}, u32[]{:S(2)}) %collective-permute-start.11) | collective-permute-done | bytes 65568 | tf_op jit(solution)/shard_map/ppermute | solution.py:148
  316.3 2.8 collective-permute-start.13
  327.4 58.4 %all_to_all.10 = bf16[64,1,10,1024]{3,2,1,0:T(8,128)(2,1)S(1)} all-to-all(bf16[64,1,10,1024]{3,2,1,0:T(8,128)(2,1)S(1)} %bitcast.221), channel_id=1, replica_groups=mesh['seq'=64,'tp'=4] {'seq'}, dimensions={0} | all-to-all | bytes 2621440 | tf_op jit(solution)/shard_map/all_to_all | solution.py:195
  387.2 2.4 fusion.48
  393.9 5.6 %all-to-all-start.1 = ((bf16[64,1,10,1024]{3,2,1,0:T(8,128)(2,1)}), bf16[64,1,10,1024]{3,2,1,0:T(8,128)(2,1)S(1)}, u32[]{:S(2)}, u32[]{:S(2)}) async-start(bf16[64,1,10,1024]{3,2,1,0:T(8,128)(2,1)} %copy.130), calls=%async_computation.1 | async-start | bytes 4194304 | tf_op jit(solution)/shard_map/all_to_all | solution.py:207
  403.4 47.3 %all-to-all-done.1 = bf16[64,1,10,1024]{3,2,1,0:T(8,128)(2,1)S(1)} async-done(((bf16[64,1,10,1024]{3,2,1,0:T(8,128)(2,1)}), bf16[64,1,10,1024]{3,2,1,0:T(8,128)(2,1)S(1)}, u32[]{:S(2)}, u32[]{:S(2)}) %all-to-all-start.1) | async-done | bytes 1310752 | tf_op jit(solution)/shard_map/all_to_all | solution.py:207
  456.0 19.3 %reduce-scatter.2.cloned.1.call-done = bf16[128,256]{1,0:T(8,128)(2,1)} async-done(((bf16[128,1024]{1,0:T(8,128)(2,1)}), bf16[128,256]{1,0:T(8,128)(2,1)}) %reduce-scatter.2.cloned.1.call-update) | async-done | bytes 65552 | tf_op jit(solution)/shard_map/reduce_scatter | solution.py:217
  (185 shorter events, 66.6 us)
Async XLA Ops:
  6.5 384.4 %copy-start = (bf16[1,352,1024]{2,1,0:T(8,128)(2,1)S(1)}, bf16[1,352,1024]{2,1,0:T(8,128)(2,1)}, u32[]{:S(2)}) copy-start(bf16[1,352,1024]{2,1,0:T(8,128)(2,1)} %param.27) | copy-start | bytes 2162692
  6.5 12.7 %copy-start.6 = (bf16[33,128,256]{2,1,0:T(8,128)(2,1)S(1)}, bf16[33,128,256]{2,1,0:T(8,128)(2,1)}, u32[]{:S(2)}) copy-start(bf16[33,128,256]{2,1,0:T(8,128)(2,1)} %param.22) | copy-start | bytes 6488068
  6.5 84.3 %all-gather.2.cloned.1.call-start = ((), (), s32[]{:S(2)}) async-start(), calls=%async_computation.3 | async-start | bytes 4259840 | tf_op jit(solution)/shard_map/all_gather | solution.py:105
  9.8 225.5 %collective-permute-start.15 = (bf16[256,1024]{1,0:T(8,128)(2,1)}, bf16[256,1024]{1,0:T(8,128)(2,1)}, u32[]{:S(2)}, u32[]{:S(2)}) collective-permute-start(bf16[256,1024]{1,0:T(8,128)(2,1)} %param.21), channel_id=1, source_target_pairs={{0,1},{1,2},{2,3},{3,0},{4,5},{5,6},{6,7},{7,4},{8,9},{9,10},{10,1... | collective-permute-start | bytes 1572872 | tf_op jit(solution)/shard_map/ppermute | solution.py:163
  11.5 223.8 %collective-permute-start.16 = (bf16[256,1024]{1,0:T(8,128)(2,1)}, bf16[256,1024]{1,0:T(8,128)(2,1)}, u32[]{:S(2)}, u32[]{:S(2)}) collective-permute-start(bf16[256,1024]{1,0:T(8,128)(2,1)} %param.21), channel_id=1, source_target_pairs={{0,2},{1,3},{2,0},{3,1},{4,6},{5,7},{6,4},{7,5},{8,10},{9,11},{10,... | collective-permute-start | bytes 1572872 | tf_op jit(solution)/shard_map/ppermute | solution.py:163
  14.4 220.9 %collective-permute-start.17 = (bf16[256,1024]{1,0:T(8,128)(2,1)}, bf16[256,1024]{1,0:T(8,128)(2,1)}, u32[]{:S(2)}, u32[]{:S(2)}) collective-permute-start(bf16[256,1024]{1,0:T(8,128)(2,1)} %param.21), channel_id=1, source_target_pairs={{0,3},{1,0},{2,1},{3,2},{4,7},{5,4},{6,5},{7,6},{8,11},{9,8},{10,9... | collective-permute-start | bytes 1572872 | tf_op jit(solution)/shard_map/ppermute | solution.py:163
  22.8 6.9 %copy-start.17 = (s32[34]{0:T(128)}, s32[34]{0:T(128)S(1)}, u32[]{:S(2)}) copy-start(s32[34]{0:T(128)S(1)} %pad_add_fusion.1) | copy-start | bytes 412
  32.1 84.4 %copy-start.16 = (s32[1024]{0:T(1024)}, s32[1024]{0:T(1024)S(1)}, u32[]{:S(2)}) copy-start(s32[1024]{0:T(1024)S(1)} %pad_clamp_fusion.1) | copy-start | bytes 12292
  141.1 17.5 %copy-start.13 = (pred[34,16]{1,0:T(8,128)(4,1)S(1)}, pred[34,16]{1,0:T(8,128)(4,1)}, u32[]{:S(2)}) copy-start(pred[34,16]{1,0:T(8,128)(4,1)} %copy.115) | copy-start | bytes 1636
  158.6 6.1 %copy-start.12 = (bf16[128,256]{0,1:T(8,128)(2,1)S(1)}, bf16[128,256]{0,1:T(8,128)(2,1)}, u32[]{:S(2)}) copy-start(bf16[128,256]{0,1:T(8,128)(2,1)} %copy.113) | copy-start | bytes 196612
  164.7 21.5 %copy-start.18 = (s32[34]{0:T(128)S(1)}, s32[34]{0:T(128)}, u32[]{:S(2)}) copy-start(s32[34]{0:T(128)} %copy-done.17) | copy-start | bytes 412
  229.9 5.4 %copy-start.15 = (s32[128,2]{0,1:T(2,128)S(1)}, s32[128,2]{0,1:T(2,128)}, u32[]{:S(2)}) copy-start(s32[128,2]{0,1:T(2,128)} %param.17) | copy-start | bytes 3076
  229.9 5.4 %copy-start.20 = (s32[128,2]{0,1:T(2,128)S(1)}, s32[128,2]{0,1:T(2,128)}, u32[]{:S(2)}) copy-start(s32[128,2]{0,1:T(2,128)} %copy.125) | copy-start | bytes 3076
  229.9 5.4 %copy-start.11 = (bf16[256,1024]{1,0:T(8,128)(2,1)S(1)}, bf16[256,1024]{1,0:T(8,128)(2,1)}, u32[]{:S(2)}) copy-start(bf16[256,1024]{1,0:T(8,128)(2,1)} %param.21) | copy-start | bytes 1572868
  235.0 11.6 %collective-permute-start.1 = (bf16[2,2,2,2,2,4,128,64]{6,7,5,4,3,2,1,0:T(8,128)(2,1)}, bf16[2,2,2,2,2,4,128,64]{6,7,5,4,3,2,1,0:T(8,128)(2,1)}, u32[]{:S(2)}, u32[]{:S(2)}) collective-permute-start(bf16[2,2,2,2,2,4,128,64]{6,7,5,4,3,2,1,0:T(8,128)(2,1)} %fusion.22), channel_id=1, source_target_pairs={{0,4},{4,0},{8,12},{12,8},{16,20},{20,16},{24,28},{28,24},{32,36},... | collective-permute-start | bytes 6291464 | tf_op jit(solution)/shard_map/ppermute | solution.py:148
  243.0 1.4 collective-permute-start
  244.6 6.5 %collective-permute-start.2 = (f32[2,2,2,2,4,128,2]{5,4,3,2,1,0,6:T(4,128)S(1)}, f32[2,2,2,2,4,128,2]{5,4,3,2,1,0,6:T(4,128)S(1)}, u32[]{:S(2)}, u32[]{:S(2)}) collective-permute-start(f32[2,2,2,2,4,128,2]{5,4,3,2,1,0,6:T(4,128)S(1)} %get-tuple-element.30), channel_id=1, source_target_pairs={{0,8},{4,12},{8,0},{12,4},{16,24},{20,28},{24,16},{28,20},{32,40},... | collective-permute-start | bytes 196616 | tf_op jit(solution)/shard_map/ppermute | solution.py:149
  250.7 25.3 %collective-permute-start.3 = (bf16[2,2,2,2,4,128,64]{5,6,4,3,2,1,0:T(8,128)(2,1)S(1)}, bf16[2,2,2,2,4,128,64]{5,6,4,3,2,1,0:T(8,128)(2,1)S(1)}, u32[]{:S(2)}, u32[]{:S(2)}) collective-permute-start(bf16[2,2,2,2,4,128,64]{5,6,4,3,2,1,0:T(8,128)(2,1)S(1)} %fusion.37), channel_id=1, source_target_pairs={{0,8},{4,12},{8,0},{12,4},{16,24},{20,28},{24,16},{28,20},{32,40},... | collective-permute-start | bytes 3145736 | tf_op jit(solution)/shard_map/ppermute | solution.py:148
  251.1 4.0 collective-permute-start.4
  255.1 22.4 %collective-permute-start.6 = (f32[2,2,4,128,2]{3,2,1,0,4:T(4,128)S(1)}, f32[2,2,4,128,2]{3,2,1,0,4:T(4,128)S(1)}, u32[]{:S(2)}, u32[]{:S(2)}) collective-permute-start(f32[2,2,4,128,2]{3,2,1,0,4:T(4,128)S(1)} %get-tuple-element.36), channel_id=1, source_target_pairs={{0,16},{4,20},{8,24},{12,28},{16,0},{20,4},{24,8},{28,12},{32,48},... | collective-permute-start | bytes 49160 | tf_op jit(solution)/shard_map/ppermute | solution.py:149
  276.8 13.1 %collective-permute-start.5 = (bf16[2,2,2,4,128,64]{4,5,3,2,1,0:T(8,128)(2,1)S(1)}, bf16[2,2,2,4,128,64]{4,5,3,2,1,0:T(8,128)(2,1)S(1)}, u32[]{:S(2)}, u32[]{:S(2)}) collective-permute-start(bf16[2,2,2,4,128,64]{4,5,3,2,1,0:T(8,128)(2,1)S(1)} %fusion.54), channel_id=1, source_target_pairs={{0,32},{4,36},{8,40},{12,44},{16,48},{20,52},{24,56},{28,60},{32,0... | collective-permute-start | bytes 1572872 | tf_op jit(solution)/shard_map/ppermute | solution.py:148
  277.6 13.4 %collective-permute-start.8 = (f32[2,4,128,2]{2,1,0,3:T(4,128)S(1)}, f32[2,4,128,2]{2,1,0,3:T(4,128)S(1)}, u32[]{:S(2)}, u32[]{:S(2)}) collective-permute-start(f32[2,4,128,2]{2,1,0,3:T(4,128)S(1)} %get-tuple-element.40), channel_id=1, source_target_pairs={{0,64},{4,68},{8,72},{12,76},{16,80},{20,84},{24,88},{28,92},{32,9... | collective-permute-start | bytes 24584 | tf_op jit(solution)/shard_map/ppermute | solution.py:149
  290.1 8.0 %collective-permute-start.7 = (bf16[2,2,4,128,64]{3,4,2,1,0:T(8,128)(2,1)S(1)}, bf16[2,2,4,128,64]{3,4,2,1,0:T(8,128)(2,1)S(1)}, u32[]{:S(2)}, u32[]{:S(2)}) collective-permute-start(bf16[2,2,4,128,64]{3,4,2,1,0:T(8,128)(2,1)S(1)} %fusion.60), channel_id=1, source_target_pairs={{0,16},{4,20},{8,24},{12,28},{16,0},{20,4},{24,8},{28,12},{32,48},... | collective-permute-start | bytes 786440 | tf_op jit(solution)/shard_map/ppermute | solution.py:148
  291.1 17.7 %collective-permute-start.10 = (f32[4,128,2]{1,0,2:T(4,128)S(1)}, f32[4,128,2]{1,0,2:T(4,128)S(1)}, u32[]{:S(2)}, u32[]{:S(2)}) collective-permute-start(f32[4,128,2]{1,0,2:T(4,128)S(1)} %get-tuple-element.47), channel_id=1, source_target_pairs={{0,128},{4,132},{8,136},{12,140},{16,144},{20,148},{24,152},{28,15... | collective-permute-start | bytes 12296 | tf_op jit(solution)/shard_map/ppermute | solution.py:149
  298.3 7.4 %collective-permute-start.9 = (bf16[2,4,128,64]{2,3,1,0:T(8,128)(2,1)S(1)}, bf16[2,4,128,64]{2,3,1,0:T(8,128)(2,1)S(1)}, u32[]{:S(2)}, u32[]{:S(2)}) collective-permute-start(bf16[2,4,128,64]{2,3,1,0:T(8,128)(2,1)S(1)} %fusion.69), channel_id=1, source_target_pairs={{0,64},{4,68},{8,72},{12,76},{16,80},{20,84},{24,88},{28,92},{32,9... | collective-permute-start | bytes 393224 | tf_op jit(solution)/shard_map/ppermute | solution.py:148
  305.8 9.0 %collective-permute-start.11 = (bf16[4,128,64]{1,2,0:T(8,128)(2,1)S(1)}, bf16[4,128,64]{1,2,0:T(8,128)(2,1)S(1)}, u32[]{:S(2)}, u32[]{:S(2)}) collective-permute-start(bf16[4,128,64]{1,2,0:T(8,128)(2,1)S(1)} %fusion.73), channel_id=1, source_target_pairs={{0,128},{4,132},{8,136},{12,140},{16,144},{20,148},{24,152},{28,15... | collective-permute-start | bytes 196616 | tf_op jit(solution)/shard_map/ppermute | solution.py:148
  314.8 6.7 %collective-permute-start.12 = (bf16[128,256]{0,1:T(8,128)(2,1)S(1)}, bf16[128,256]{0,1:T(8,128)(2,1)S(1)}, u32[]{:S(2)}, u32[]{:S(2)}) collective-permute-start(bf16[128,256]{0,1:T(8,128)(2,1)S(1)} %bitcast.233), channel_id=1, source_target_pairs={{0,1},{1,2},{2,3},{3,0},{4,5},{5,6},{6,7},{7,4},{8,9},{9,10},{10,1... | collective-permute-start | bytes 196616 | tf_op jit(solution)/shard_map/ppermute | solution.py:163
  316.3 5.8 %collective-permute-start.13 = (bf16[128,256]{0,1:T(8,128)(2,1)S(1)}, bf16[128,256]{0,1:T(8,128)(2,1)S(1)}, u32[]{:S(2)}, u32[]{:S(2)}) collective-permute-start(bf16[128,256]{0,1:T(8,128)(2,1)S(1)} %bitcast.234), channel_id=1, source_target_pairs={{0,2},{1,3},{2,0},{3,1},{4,6},{5,7},{6,4},{7,5},{8,10},{9,11},{10,... | collective-permute-start | bytes 196616 | tf_op jit(solution)/shard_map/ppermute | solution.py:163
  319.1 4.3 collective-permute-start.14
  393.9 5.9 %copy-start.5 = (f32[128,1024]{1,0:T(8,128)S(1)}, f32[128,1024]{1,0:T(8,128)}, u32[]{:S(2)}) copy-start(f32[128,1024]{1,0:T(8,128)} %copy-done.4) | copy-start | bytes 1572868
  393.9 56.8 %all-to-all-start.1 = ((bf16[64,1,10,1024]{3,2,1,0:T(8,128)(2,1)}), bf16[64,1,10,1024]{3,2,1,0:T(8,128)(2,1)S(1)}, u32[]{:S(2)}, u32[]{:S(2)}) async-start(bf16[64,1,10,1024]{3,2,1,0:T(8,128)(2,1)} %copy.130), calls=%async_computation.1 | async-start | bytes 4194304 | tf_op jit(solution)/shard_map/all_to_all | solution.py:207
  399.5 75.8 %reduce-scatter.2.cloned.1.call-start = ((), (), s32[]{:S(2)}) async-start(), calls=%async_computation.4 | async-start | bytes 327680 | tf_op jit(solution)/shard_map/reduce_scatter | solution.py:217
  (12 other events, 32.9 us)
Sparse Core Ops, SparseCore 0:
  10.1 80.6 all-gather.1
  456.1 19.1 reduce-scatter.1
where the time goes:
time: 488 us; the launch traced here: 484 us
  waiting for transfers between devices  173 us (35%)
  local copies, waits for them, and re-layouts  87.9 us (18%)
  matrix products  77.9 us (16%)
  blocking collectives  58.4 us (12%)
  other arithmetic  37.1 us (8%)
  starting transfers between devices  35 us (7%)
  between operations  14.4 us (3%)
    all_to_all x1, blocking collectives, shards(): lax.all_to_all(outgoing, 'seq', split_axis=0, concat_axis=0, tiled=True)  58.4 us
    all_gather x1, waiting for transfers between devices, shards(): lax.all_gather(queries, 'seq', axis=0, tiled=True)  56.6 us
    all_to_all x1, waiting for transfers between devices, shards(): lax.all_to_all(produced.astype(jnp.bfloat16), 'seq', split_axis=0, concat...  47.3 us
    ppermute x6, waiting for transfers between devices, shards(): lax.ppermute(send_acc.astype(jnp.bfloat16), 'seq', pairs)  44.2 us
    reshape x2, local copies, waits for them, and re-layouts, shards(): lax.all_gather(queries, 'seq', axis=0, tiled=True)  25.7 us
    dot_general x1, matrix products, shards(): jnp.einsum('br,bhqd->rhqd', weights, acc_block * factor[..., None], preci...  25.1 us
    dot_general x1, matrix products, shards(): jnp.einsum('bhqk,bkhd->bhqd', probs.astype(jnp.bfloat16), values, preferr...  21.5 us
    reduce_scatter x1, waiting for transfers between devices, shards(): lax.psum_scatter(mixture.astype(jnp.bfloat16), 'tp', scatter_dimension=1,...  19.3 us
  transfers between devices with their start and end apart: 21, of which 12 were waited for; matrix products, arithmetic and copies ran while one was open for 37% of the time, Pallas kernels for 0%

commit v1 on v0

--- a/solution.py
+++ b/solution.py
@@ -102,9 +102,9 @@
     values = jnp.concatenate(
         [cache_v.reshape(page_count, PAGE, local_heads, DH), new_values[None]], axis=0
     )
-    everyone = lax.all_gather(queries, "seq", axis=0, tiled=True).reshape(
-        request_total, span_rows, local_heads, DH
-    )
+    everyone = jnp.concatenate(
+        lax.all_to_all(jnp.stack([queries] * lax.axis_size("seq")), "seq", 0, 0), axis=0
+    ).reshape(request_total, span_rows, local_heads, DH)
     rows = everyone[jnp.maximum(owners, 0)]
     scores = jnp.einsum("bqhd,bkhd->bhqk", rows, keys, preferred_element_type=jnp.float32) * DH ** (
         -0.5

time: 488 us -> 512 us (1.049)
  waiting for transfers between devices: 173 us -> 196 us
  starting transfers between devices: 35 us -> 40.4 us
    all_to_all x0 -> x1, waiting for transfers between devices: none -> 73.1 us  [shards(): lax.all_to_all(jnp.stack([queries] * lax.axis_size('seq')), 'seq', 0, 0)]
    all_gather x1 -> x0, waiting for transfers between devices: 56.6 us -> none  [shards(): lax.all_gather(queries, 'seq', axis=0, tiled=True)]
    reshape x2 -> x0, local copies, waits for them, and re-layouts: 25.7 us -> none  [shards(): lax.all_gather(queries, 'seq', axis=0, tiled=True)]
    another operation x1 -> x4, local copies, waits for them, and re-layouts: 0.01 us -> 17.1 us  [the longest x2 14.1 us: shards(): everyone = jnp.concatenate(lax.all_to_all(jnp.stack([queries] * lax.axis_...]
    all_to_all x0 -> x1, starting transfers between devices: none -> 12.3 us  [shards(): lax.all_to_all(jnp.stack([queries] * lax.axis_size('seq')), 'seq', 0, 0)]
    all_to_all x0 -> x1, local copies, waits for them, and re-layouts: none -> 6.91 us  [shards(): lax.all_to_all(jnp.stack([queries] * lax.axis_size('seq')), 'seq', 0, 0)]
    ppermute x6, starting transfers between devices: 10.2 us -> 4.81 us  [shards(): got_stats = lax.ppermute(send_stats, 'seq', pairs)]
    ppermute x6, waiting for transfers between devices: 44.2 us -> 49.5 us  [shards(): lax.ppermute(send_acc.astype(jnp.bfloat16), 'seq', pairs)]
  transfers between devices with their start and end apart: 21 -> 21, of which waited for: 12 -> 13; matrix products, arithmetic and copies ran while one was open for 37% -> 34% of each run, Pallas kernels for 0% -> 0%
where the time goes in v1:
time: 512 us; the launch traced here: 507 us
  waiting for transfers between devices  196 us (38%)
  local copies, waits for them, and re-layouts  84.7 us (17%)
  matrix products  77 us (15%)
  blocking collectives  57.3 us (11%)
  starting transfers between devices  40.4 us (8%)
  other arithmetic  37.5 us (7%)
  between operations  14.5 us (3%)
    all_to_all x1, waiting for transfers between devices, shards(): lax.all_to_all(jnp.stack([queries] * lax.axis_size('seq')), 'seq', 0, 0)  73.1 us
    all_to_all x1, blocking collectives, shards(): lax.all_to_all(outgoing, 'seq', split_axis=0, concat_axis=0, tiled=True)  57.3 us
    ppermute x6, waiting for transfers between devices, shards(): lax.ppermute(send_acc.astype(jnp.bfloat16), 'seq', pairs)  49.5 us
    all_to_all x1, waiting for transfers between devices, shards(): lax.all_to_all(produced.astype(jnp.bfloat16), 'seq', split_axis=0, concat...  47.3 us
    dot_general x1, matrix products, shards(): jnp.einsum('br,bhqd->rhqd', weights, acc_block * factor[..., None], preci...  24.9 us
    dot_general x1, matrix products, shards(): jnp.einsum('bhqk,bkhd->bhqd', probs.astype(jnp.bfloat16), values, preferr...  21.5 us
    reduce_scatter x1, waiting for transfers between devices, shards(): lax.psum_scatter(mixture.astype(jnp.bfloat16), 'tp', scatter_dimension=1,...  19.3 us
    reduce_sum x1, other arithmetic, shards(): l_block = jnp.sum(probs, axis=-1)  17.9 us
  transfers between devices with their start and end apart: 21, of which 13 were waited for; matrix products, arithmetic and copies ran while one was open for 34% of the time, Pallas kernels for 0%

profile of v1, /device:TPU:2, one launch (start us, length us, event | category | flops | bytes accessed | tf_op | source)
XLA Modules:
  0.0 506.8 jit_solution(16037547418997433374)
XLA Ops:
  9.2 3.0 stack.36
  12.3 12.3 %all-to-all-start = ((bf16[64,128,256]{1,2,0:T(8,128)(2,1)}), bf16[64,128,256]{1,2,0:T(8,128)(2,1)}, u32[]{:S(2)}, u32[]{:S(2)}) async-start(bf16[64,128,256]{1,2,0:T(8,128)(2,1)} %stack.36), calls=%async_computation | async-start | bytes 8388608 | tf_op jit(solution)/shard_map/all_to_all | solution.py:106
  26.3 2.9 collective-permute-start.16
  32.6 2.4 copy.113
  38.9 4.1 copy.115
  47.6 73.1 %all-to-all-done = bf16[64,128,256]{1,2,0:T(8,128)(2,1)} async-done(((bf16[64,128,256]{1,2,0:T(8,128)(2,1)}), bf16[64,128,256]{1,2,0:T(8,128)(2,1)}, u32[]{:S(2)}, u32[]{:S(2)}) %all-to-all-start) | async-done | bytes 4194336 | tf_op jit(solution)/shard_map/all_to_all | solution.py:106
  120.7 6.9 %copy.111 = bf16[64,128,256]{1,0,2:T(8,128)(2,1)} copy(bf16[64,128,256]{1,2,0:T(8,128)(2,1)} %all-to-all-done) | data formatting | bytes 8388608 | tf_op jit(solution)/shard_map/all_to_all | solution.py:106
  127.6 7.5 %reshape_reshape.6 = bf16[16,512,4,64]{1,0,3,2:T(8,128)(2,1)} reshape(bf16[64,128,256]{1,0,2:T(8,128)(2,1)} %copy.111) | data formatting | bytes 8388608 | tf_op jit(solution)/shard_map/reshape;reshape | solution.py:107
  135.2 6.6 %copy.112 = bf16[16,512,4,64]{1,3,2,0:T(8,128)(2,1)} copy(bf16[16,512,4,64]{1,0,3,2:T(8,128)(2,1)} %reshape_reshape.6) | data formatting | bytes 8388608 | tf_op jit(solution)/shard_map/reshape;reshape | solution.py:107
  141.7 7.5 %gather_fusion.1 = bf16[34,512,4,64]{1,3,2,0:T(8,128)(2,1)} fusion(bf16[16,512,4,64]{1,3,2,0:T(8,128)(2,1)} %copy.112, s32[1024]{0:T(1024)S(1)} %pad_clamp_fusion.1), kind=kCustom, calls=%fused_computation.1 | custom fusion | bytes 17825928 | tf_op jit(solution)/shard_map/gather | solution.py:108
  149.2 17.1 %fusion = (f32[34,4,512]{2,1,0:T(4,128)S(1)}, f32[34,4,512,128]{2,3,1,0:T(8,128)}) fusion(pred[34,512,128]{1,2,0:T(8,128)(4,1)S(1)} %pad_add_fusion, bf16[34,512,4,64]{1,3,2,0:T(8,128)(2,1)} %gather_fusion.1, bf16[1,128,4,64]{1,3,2,0:T(8,128)(2,1)S(1)} %bitcast.240, bf16[33,128,4,64]{1,3,2,0:T(8,128)(2,1)} %bitcast.225), kind=kOutput, calls=%fused_computation.8 | convolution fusion | flops 1168633856 | bytes 49299456 | tf_op jit(solution)/shard_map/bqhd,bkhd->bhqk/dot_general | solution.py:109
  166.3 17.9 %fusion.1 = f32[34,4,512]{2,1,0:T(4,128)} fusion(f32[34,4,512,128]{2,3,1,0:T(8,128)} %get-tuple-element.56, f32[34,4,512]{2,1,0:T(4,128)S(1)} %get-tuple-element.55, pred[34,512,128]{1,2,0:T(8,128)(4,1)S(1)} %pad_add_fusion), kind=kLoop, calls=%fused_computation.9 | loop fusion | flops 44494848 | bytes 38436864 | tf_op jit(solution)/shard_map/reduce_sum | solution.py:115
  186.0 2.5 gather_fusion.2
  190.3 21.5 %broadcast_multiply_fusion = f32[34,4,512,64]{2,3,1,0:T(8,128)} fusion(f32[34,4,512]{2,1,0:T(4,128)S(1)} %bitcast.234, f32[34,4,512,128]{2,3,1,0:T(8,128)} %get-tuple-element.56, f32[34,4,512]{2,1,0:T(4,128)S(1)} %get-tuple-element.55, pred[34,512,128]{1,2,0:T(8,128)(4,1)S(1)} %pad_add_fusion, bf16[1,128,4,64]{1,3,2,0:T(8,128)(2,1)S(1)} %bitcast.241, ...), kind=kOutput, calls=%fused_computation.19 | convolution fusion | flops 1194328064 | bytes 58490880 | tf_op jit(solution)/shard_map/bhqk,bkhd->bhqd/dot_general | solution.py:116
  211.8 24.9 %fusion.3 = f32[16,4,512,64]{2,0,3,1:T(8,128)} fusion(f32[34,4,512,64]{2,3,1,0:T(8,128)} %broadcast_multiply_fusion, s32[34]{0:T(128)S(1)} %copy-done.20), kind=kOutput, calls=%fused_computation.11 | convolution fusion | flops 855638528 | bytes 26214536 | tf_op jit(solution)/shard_map/br,bhqd->rhqd/dot_general | solution.py:123
  236.7 10.1 %reshape.407 = f32[16,4,4,128,64]{3,2,0,4,1:T(4,128)} reshape(f32[16,4,512,64]{2,0,3,1:T(8,128)} %fusion.3) | data formatting | bytes 16777216 | tf_op jit(solution)/shard_map/reshape | solution.py:129
  246.8 8.2 %copy.121 = f32[16,4,4,128,64]{3,4,2,1,0:T(8,128)S(1)} copy(f32[16,4,4,128,64]{3,1,0,4,2:T(4,128)} %bitcast.219) | data formatting | bytes 16777216 | tf_op jit(solution)/shard_map/transpose | solution.py:128
  255.1 3.2 copy-done.2
  260.3 2.9 pad_maximum_fusion
  270.5 4.0 fusion.14
  276.8 3.4 collective-permute-done.4
  282.6 17.5 %collective-permute-done.3 = bf16[2,2,2,2,4,128,64]{5,6,4,3,2,1,0:T(8,128)(2,1)S(1)} collective-permute-done((bf16[2,2,2,2,4,128,64]{5,6,4,3,2,1,0:T(8,128)(2,1)S(1)}, bf16[2,2,2,2,4,128,64]{5,6,4,3,2,1,0:T(8,128)(2,1)S(1)}, u32[]{:S(2)}, u32[]{:S(2)}) %collective-permute-start.3) | collective-permute-done | bytes 1048608 | tf_op jit(solution)/shard_map/ppermute | solution.py:148
  302.1 11.8 %collective-permute-done.5 = bf16[2,2,2,4,128,64]{4,5,3,2,1,0:T(8,128)(2,1)S(1)} collective-permute-done((bf16[2,2,2,4,128,64]{4,5,3,2,1,0:T(8,128)(2,1)S(1)}, bf16[2,2,2,4,128,64]{4,5,3,2,1,0:T(8,128)(2,1)S(1)}, u32[]{:S(2)}, u32[]{:S(2)}) %collective-permute-start.5) | collective-permute-done | bytes 524320 | tf_op jit(solution)/shard_map/ppermute | solution.py:148
  316.7 5.7 %collective-permute-done.7 = bf16[2,2,4,128,64]{3,4,2,1,0:T(8,128)(2,1)S(1)} collective-permute-done((bf16[2,2,4,128,64]{3,4,2,1,0:T(8,128)(2,1)S(1)}, bf16[2,2,4,128,64]{3,4,2,1,0:T(8,128)(2,1)S(1)}, u32[]{:S(2)}, u32[]{:S(2)}) %collective-permute-start.7) | collective-permute-done | bytes 262176 | tf_op jit(solution)/shard_map/ppermute | solution.py:148
  322.6 7.0 %collective-permute-done.9 = bf16[2,4,128,64]{2,3,1,0:T(8,128)(2,1)S(1)} collective-permute-done((bf16[2,4,128,64]{2,3,1,0:T(8,128)(2,1)S(1)}, bf16[2,4,128,64]{2,3,1,0:T(8,128)(2,1)S(1)}, u32[]{:S(2)}, u32[]{:S(2)}) %collective-permute-start.9) | collective-permute-done | bytes 131104 | tf_op jit(solution)/shard_map/ppermute | solution.py:148
  331.0 7.6 %collective-permute-done.11 = bf16[4,128,64]{1,2,0:T(8,128)(2,1)S(1)} collective-permute-done((bf16[4,128,64]{1,2,0:T(8,128)(2,1)S(1)}, bf16[4,128,64]{1,2,0:T(8,128)(2,1)S(1)}, u32[]{:S(2)}, u32[]{:S(2)}) %collective-permute-start.11) | collective-permute-done | bytes 65568 | tf_op jit(solution)/shard_map/ppermute | solution.py:148
  340.2 2.9 collective-permute-start.13
  351.5 57.3 %all_to_all.15 = bf16[64,1,10,1024]{3,2,1,0:T(8,128)(2,1)S(1)} all-to-all(bf16[64,1,10,1024]{3,2,1,0:T(8,128)(2,1)S(1)} %bitcast.223), channel_id=1, replica_groups=mesh['seq'=64,'tp'=4] {'seq'}, dimensions={0} | all-to-all | bytes 2621440 | tf_op jit(solution)/shard_map/all_to_all | solution.py:195
  410.1 2.4 fusion.48
  416.9 5.6 %all-to-all-start.2 = ((bf16[64,1,10,1024]{3,2,1,0:T(8,128)(2,1)}), bf16[64,1,10,1024]{3,2,1,0:T(8,128)(2,1)S(1)}, u32[]{:S(2)}, u32[]{:S(2)}) async-start(bf16[64,1,10,1024]{3,2,1,0:T(8,128)(2,1)} %copy.133), calls=%async_computation.2 | async-start | bytes 4194304 | tf_op jit(solution)/shard_map/all_to_all | solution.py:207
  426.4 47.3 %all-to-all-done.2 = bf16[64,1,10,1024]{3,2,1,0:T(8,128)(2,1)S(1)} async-done(((bf16[64,1,10,1024]{3,2,1,0:T(8,128)(2,1)}), bf16[64,1,10,1024]{3,2,1,0:T(8,128)(2,1)S(1)}, u32[]{:S(2)}, u32[]{:S(2)}) %all-to-all-start.2) | async-done | bytes 1310752 | tf_op jit(solution)/shard_map/all_to_all | solution.py:207
  479.0 19.3 %reduce-scatter.2.cloned.1.call-done = bf16[128,256]{1,0:T(8,128)(2,1)} async-done(((bf16[128,1024]{1,0:T(8,128)(2,1)}), bf16[128,256]{1,0:T(8,128)(2,1)}) %reduce-scatter.2.cloned.1.call-update) | async-done | bytes 65552 | tf_op jit(solution)/shard_map/reduce_scatter | solution.py:217
  (191 shorter events, 66.1 us)
Async XLA Ops:
  6.5 407.3 %copy-start = (bf16[1,352,1024]{2,1,0:T(8,128)(2,1)S(1)}, bf16[1,352,1024]{2,1,0:T(8,128)(2,1)}, u32[]{:S(2)}) copy-start(bf16[1,352,1024]{2,1,0:T(8,128)(2,1)} %param.27) | copy-start | bytes 2162692
  12.3 18.4 %copy-start.15 = (s32[128,2]{0,1:T(2,128)S(1)}, s32[128,2]{0,1:T(2,128)}, u32[]{:S(2)}) copy-start(s32[128,2]{0,1:T(2,128)} %param.17) | copy-start | bytes 3076
  12.3 18.8 %copy-start.17 = (s32[16,256]{1,0:T(8,128)S(1)}, s32[16,256]{1,0:T(8,128)}, u32[]{:S(2)}) copy-start(s32[16,256]{1,0:T(8,128)} %param.15) | copy-start | bytes 49156
  12.3 18.9 %copy-start.3 = (bf16[128,1024]{1,0:T(8,128)(2,1)S(1)}, bf16[128,1024]{1,0:T(8,128)(2,1)}, u32[]{:S(2)}) copy-start(bf16[128,1024]{1,0:T(8,128)(2,1)} %param.14) | copy-start | bytes 786436
  12.3 20.3 %copy-start.6 = (bf16[33,128,256]{2,1,0:T(8,128)(2,1)S(1)}, bf16[33,128,256]{2,1,0:T(8,128)(2,1)}, u32[]{:S(2)}) copy-start(bf16[33,128,256]{2,1,0:T(8,128)(2,1)} %param.22) | copy-start | bytes 6488068
  12.3 108.5 %all-to-all-start = ((bf16[64,128,256]{1,2,0:T(8,128)(2,1)}), bf16[64,128,256]{1,2,0:T(8,128)(2,1)}, u32[]{:S(2)}, u32[]{:S(2)}) async-start(bf16[64,128,256]{1,2,0:T(8,128)(2,1)} %stack.36), calls=%async_computation | async-start | bytes 8388608 | tf_op jit(solution)/shard_map/all_to_all | solution.py:106
  24.6 235.6 %collective-permute-start.15 = (bf16[256,1024]{1,0:T(8,128)(2,1)}, bf16[256,1024]{1,0:T(8,128)(2,1)}, u32[]{:S(2)}, u32[]{:S(2)}) collective-permute-start(bf16[256,1024]{1,0:T(8,128)(2,1)} %param.21), channel_id=1, source_target_pairs={{0,1},{1,2},{2,3},{3,0},{4,5},{5,6},{6,7},{7,4},{8,9},{9,10},{10,1... | collective-permute-start | bytes 1572872 | tf_op jit(solution)/shard_map/ppermute | solution.py:163
  26.3 234.0 %collective-permute-start.16 = (bf16[256,1024]{1,0:T(8,128)(2,1)}, bf16[256,1024]{1,0:T(8,128)(2,1)}, u32[]{:S(2)}, u32[]{:S(2)}) collective-permute-start(bf16[256,1024]{1,0:T(8,128)(2,1)} %param.21), channel_id=1, source_target_pairs={{0,2},{1,3},{2,0},{3,1},{4,6},{5,7},{6,4},{7,5},{8,10},{9,11},{10,... | collective-permute-start | bytes 1572872 | tf_op jit(solution)/shard_map/ppermute | solution.py:163
  29.2 231.1 %collective-permute-start.17 = (bf16[256,1024]{1,0:T(8,128)(2,1)}, bf16[256,1024]{1,0:T(8,128)(2,1)}, u32[]{:S(2)}, u32[]{:S(2)}) collective-permute-start(bf16[256,1024]{1,0:T(8,128)(2,1)} %param.21), channel_id=1, source_target_pairs={{0,3},{1,0},{2,1},{3,2},{4,7},{5,4},{6,5},{7,6},{8,11},{9,8},{10,9... | collective-permute-start | bytes 1572872 | tf_op jit(solution)/shard_map/ppermute | solution.py:163
  36.2 6.9 %copy-start.19 = (s32[34]{0:T(128)}, s32[34]{0:T(128)S(1)}, u32[]{:S(2)}) copy-start(s32[34]{0:T(128)S(1)} %pad_add_fusion.1) | copy-start | bytes 412
  45.4 96.3 %copy-start.18 = (s32[1024]{0:T(1024)}, s32[1024]{0:T(1024)S(1)}, u32[]{:S(2)}) copy-start(s32[1024]{0:T(1024)S(1)} %pad_clamp_fusion.1) | copy-start | bytes 12292
  166.3 17.9 %copy-start.13 = (pred[34,16]{1,0:T(8,128)(4,1)S(1)}, pred[34,16]{1,0:T(8,128)(4,1)}, u32[]{:S(2)}) copy-start(pred[34,16]{1,0:T(8,128)(4,1)} %copy.118) | copy-start | bytes 1636
  184.2 6.1 %copy-start.12 = (bf16[128,256]{0,1:T(8,128)(2,1)S(1)}, bf16[128,256]{0,1:T(8,128)(2,1)}, u32[]{:S(2)}) copy-start(bf16[128,256]{0,1:T(8,128)(2,1)} %copy.116) | copy-start | bytes 196612
  190.3 21.5 %copy-start.20 = (s32[34]{0:T(128)S(1)}, s32[34]{0:T(128)}, u32[]{:S(2)}) copy-start(s32[34]{0:T(128)} %copy-done.19) | copy-start | bytes 412
  260.1 10.3 %collective-permute-start.1 = (bf16[2,2,2,2,2,4,128,64]{6,7,5,4,3,2,1,0:T(8,128)(2,1)}, bf16[2,2,2,2,2,4,128,64]{6,7,5,4,3,2,1,0:T(8,128)(2,1)}, u32[]{:S(2)}, u32[]{:S(2)}) collective-permute-start(bf16[2,2,2,2,2,4,128,64]{6,7,5,4,3,2,1,0:T(8,128)(2,1)} %fusion.22), channel_id=1, source_target_pairs={{0,4},{4,0},{8,12},{12,8},{16,20},{20,16},{24,28},{28,24},{32,36},... | collective-permute-start | bytes 6291464 | tf_op jit(solution)/shard_map/ppermute | solution.py:148
  268.0 1.6 collective-permute-start
  269.7 6.5 %collective-permute-start.2 = (f32[2,2,2,2,4,128,2]{5,4,3,2,1,0,6:T(4,128)S(1)}, f32[2,2,2,2,4,128,2]{5,4,3,2,1,0,6:T(4,128)S(1)}, u32[]{:S(2)}, u32[]{:S(2)}) collective-permute-start(f32[2,2,2,2,4,128,2]{5,4,3,2,1,0,6:T(4,128)S(1)} %get-tuple-element.30), channel_id=1, source_target_pairs={{0,8},{4,12},{8,0},{12,4},{16,24},{20,28},{24,16},{28,20},{32,40},... | collective-permute-start | bytes 196616 | tf_op jit(solution)/shard_map/ppermute | solution.py:149
  274.7 25.4 %collective-permute-start.3 = (bf16[2,2,2,2,4,128,64]{5,6,4,3,2,1,0:T(8,128)(2,1)S(1)}, bf16[2,2,2,2,4,128,64]{5,6,4,3,2,1,0:T(8,128)(2,1)S(1)}, u32[]{:S(2)}, u32[]{:S(2)}) collective-permute-start(bf16[2,2,2,2,4,128,64]{5,6,4,3,2,1,0:T(8,128)(2,1)S(1)} %fusion.37), channel_id=1, source_target_pairs={{0,8},{4,12},{8,0},{12,4},{16,24},{20,28},{24,16},{28,20},{32,40},... | collective-permute-start | bytes 3145736 | tf_op jit(solution)/shard_map/ppermute | solution.py:148
  276.2 4.0 collective-permute-start.4
  280.2 21.4 %collective-permute-start.6 = (f32[2,2,4,128,2]{3,2,1,0,4:T(4,128)S(1)}, f32[2,2,4,128,2]{3,2,1,0,4:T(4,128)S(1)}, u32[]{:S(2)}, u32[]{:S(2)}) collective-permute-start(f32[2,2,4,128,2]{3,2,1,0,4:T(4,128)S(1)} %get-tuple-element.36), channel_id=1, source_target_pairs={{0,16},{4,20},{8,24},{12,28},{16,0},{20,4},{24,8},{28,12},{32,48},... | collective-permute-start | bytes 49160 | tf_op jit(solution)/shard_map/ppermute | solution.py:149
  300.8 13.1 %collective-permute-start.5 = (bf16[2,2,2,4,128,64]{4,5,3,2,1,0:T(8,128)(2,1)S(1)}, bf16[2,2,2,4,128,64]{4,5,3,2,1,0:T(8,128)(2,1)S(1)}, u32[]{:S(2)}, u32[]{:S(2)}) collective-permute-start(bf16[2,2,2,4,128,64]{4,5,3,2,1,0:T(8,128)(2,1)S(1)} %fusion.54), channel_id=1, source_target_pairs={{0,32},{4,36},{8,40},{12,44},{16,48},{20,52},{24,56},{28,60},{32,0... | collective-permute-start | bytes 1572872 | tf_op jit(solution)/shard_map/ppermute | solution.py:148
  301.7 14.8 %collective-permute-start.8 = (f32[2,4,128,2]{2,1,0,3:T(4,128)S(1)}, f32[2,4,128,2]{2,1,0,3:T(4,128)S(1)}, u32[]{:S(2)}, u32[]{:S(2)}) collective-permute-start(f32[2,4,128,2]{2,1,0,3:T(4,128)S(1)} %get-tuple-element.40), channel_id=1, source_target_pairs={{0,64},{4,68},{8,72},{12,76},{16,80},{20,84},{24,88},{28,92},{32,9... | collective-permute-start | bytes 24584 | tf_op jit(solution)/shard_map/ppermute | solution.py:149
  314.2 8.1 %collective-permute-start.7 = (bf16[2,2,4,128,64]{3,4,2,1,0:T(8,128)(2,1)S(1)}, bf16[2,2,4,128,64]{3,4,2,1,0:T(8,128)(2,1)S(1)}, u32[]{:S(2)}, u32[]{:S(2)}) collective-permute-start(bf16[2,2,4,128,64]{3,4,2,1,0:T(8,128)(2,1)S(1)} %fusion.60), channel_id=1, source_target_pairs={{0,16},{4,20},{8,24},{12,28},{16,0},{20,4},{24,8},{28,12},{32,48},... | collective-permute-start | bytes 786440 | tf_op jit(solution)/shard_map/ppermute | solution.py:148
  316.6 14.4 %collective-permute-start.10 = (f32[4,128,2]{1,0,2:T(4,128)S(1)}, f32[4,128,2]{1,0,2:T(4,128)S(1)}, u32[]{:S(2)}, u32[]{:S(2)}) collective-permute-start(f32[4,128,2]{1,0,2:T(4,128)S(1)} %get-tuple-element.47), channel_id=1, source_target_pairs={{0,128},{4,132},{8,136},{12,140},{16,144},{20,148},{24,152},{28,15... | collective-permute-start | bytes 12296 | tf_op jit(solution)/shard_map/ppermute | solution.py:149
  322.5 7.1 %collective-permute-start.9 = (bf16[2,4,128,64]{2,3,1,0:T(8,128)(2,1)S(1)}, bf16[2,4,128,64]{2,3,1,0:T(8,128)(2,1)S(1)}, u32[]{:S(2)}, u32[]{:S(2)}) collective-permute-start(bf16[2,4,128,64]{2,3,1,0:T(8,128)(2,1)S(1)} %fusion.69), channel_id=1, source_target_pairs={{0,64},{4,68},{8,72},{12,76},{16,80},{20,84},{24,88},{28,92},{32,9... | collective-permute-start | bytes 393224 | tf_op jit(solution)/shard_map/ppermute | solution.py:148
  329.7 8.9 %collective-permute-start.11 = (bf16[4,128,64]{1,2,0:T(8,128)(2,1)S(1)}, bf16[4,128,64]{1,2,0:T(8,128)(2,1)S(1)}, u32[]{:S(2)}, u32[]{:S(2)}) collective-permute-start(bf16[4,128,64]{1,2,0:T(8,128)(2,1)S(1)} %fusion.73), channel_id=1, source_target_pairs={{0,128},{4,132},{8,136},{12,140},{16,144},{20,148},{24,152},{28,15... | collective-permute-start | bytes 196616 | tf_op jit(solution)/shard_map/ppermute | solution.py:148
  338.6 6.9 %collective-permute-start.12 = (bf16[128,256]{0,1:T(8,128)(2,1)S(1)}, bf16[128,256]{0,1:T(8,128)(2,1)S(1)}, u32[]{:S(2)}, u32[]{:S(2)}) collective-permute-start(bf16[128,256]{0,1:T(8,128)(2,1)S(1)} %bitcast.235), channel_id=1, source_target_pairs={{0,1},{1,2},{2,3},{3,0},{4,5},{5,6},{6,7},{7,4},{8,9},{9,10},{10,1... | collective-permute-start | bytes 196616 | tf_op jit(solution)/shard_map/ppermute | solution.py:163
  340.2 5.8 %collective-permute-start.13 = (bf16[128,256]{0,1:T(8,128)(2,1)S(1)}, bf16[128,256]{0,1:T(8,128)(2,1)S(1)}, u32[]{:S(2)}, u32[]{:S(2)}) collective-permute-start(bf16[128,256]{0,1:T(8,128)(2,1)S(1)} %bitcast.236), channel_id=1, source_target_pairs={{0,2},{1,3},{2,0},{3,1},{4,6},{5,7},{6,4},{7,5},{8,10},{9,11},{10,... | collective-permute-start | bytes 196616 | tf_op jit(solution)/shard_map/ppermute | solution.py:163
  343.1 4.3 collective-permute-start.14
  416.9 5.9 %copy-start.5 = (f32[128,1024]{1,0:T(8,128)S(1)}, f32[128,1024]{1,0:T(8,128)}, u32[]{:S(2)}) copy-start(f32[128,1024]{1,0:T(8,128)} %copy-done.4) | copy-start | bytes 1572868
  416.9 56.8 %all-to-all-start.2 = ((bf16[64,1,10,1024]{3,2,1,0:T(8,128)(2,1)}), bf16[64,1,10,1024]{3,2,1,0:T(8,128)(2,1)S(1)}, u32[]{:S(2)}, u32[]{:S(2)}) async-start(bf16[64,1,10,1024]{3,2,1,0:T(8,128)(2,1)} %copy.133), calls=%async_computation.2 | async-start | bytes 4194304 | tf_op jit(solution)/shard_map/all_to_all | solution.py:207
  422.4 75.8 %reduce-scatter.2.cloned.1.call-start = ((), (), s32[]{:S(2)}) async-start(), calls=%async_computation.4 | async-start | bytes 327680 | tf_op jit(solution)/shard_map/reduce_scatter | solution.py:217
  (14 other events, 43.9 us)
Sparse Core Ops, SparseCore 0:
  479.1 19.1 reduce-scatter.1
